TPU v7x, 32 devices: a whole 2x2x4 slice. The times are simulated.
32 devices in a mesh: seq: 8 (over z, x), tp: 4 (over y, core).
Axes of the slice: x: 2, y: 2, z: 4, core: 2. Of those that a mesh axis runs over, the one named last changes fastest.
Arguments:
- hidden: bfloat16 [2048, 2048], P('seq', 'tp'), may hold values from -40 to 40
- new_queries: bfloat16 [2048, 2048], P('seq', 'tp'), may hold values from -9 to 9
- new_keys: bfloat16 [2048, 2048], P('seq', 'tp'), may hold values from -6 to 6
- new_values: bfloat16 [2048, 2048], P('seq', 'tp'), may hold values from -6 to 6
- cache_keys: bfloat16 [8, 4096, 2048], P('seq', None, 'tp'), may hold values from -6 to 6
- cache_values: bfloat16 [8, 4096, 2048], P('seq', None, 'tp'), may hold values from -6 to 6
- cache_lengths: int32 [8], replicated, may hold values from 1 to 4096, as said below
- out_proj: bfloat16 [2048, 2048], P('tp'), may hold values from -0.5 to 0.5
- moe_gain: float32 [2048], P('tp'), may hold values from 0.1 to 1.9
- expert_ids: int32 [2048, 8], P('seq'), may hold values from 0 to 15, all different within a row; in each aligned block of 256 rows (0 to 255, 256 to 511, ...) at most 192 rows name the same one
- route_weights: float32 [2048, 8], P('seq'), may hold values from 0.25 to 0.5
- expert_gate_up: bfloat16 [16, 2048, 2, 1024], P('seq', None, None, 'tp'), may hold values from -0.125 to 0.125
- expert_down: bfloat16 [16, 1024, 2048], P('seq', 'tp'), may hold values from -0.375 to 0.375
- next_gain: float32 [2048], P('tp'), may hold values from 0.1 to 1.9
- qkv_proj: bfloat16 [2048, 3, 2048], P(None, None, 'tp'), may hold values from -0.125 to 0.125
- query_gain: float32 [2048], P('tp'), may hold values from 0.1 to 1.9
- key_gain: float32 [2048], P('tp'), may hold values from 0.1 to 1.9
Outputs:
- layer_out: bfloat16 [2048, 2048], P('seq', 'tp')
- next_query: bfloat16 [2048, 2048], P('seq', 'tp')
- next_key: bfloat16 [2048, 2048], P('seq', 'tp')
- next_value: bfloat16 [2048, 2048], P('seq', 'tp')
Inputs may be any that keep to these rules, and one draw needn't show every extreme that they name: Request r has cached positions 0 to cache_lengths[r] - 1; one request has 4096 of them and one has 1. `expert_ids`: each row names 8 different experts; among the 256 rows of one request no expert is named more than 192 times, and in some request one expert is named exactly 192 times.
All inputs are finite; a program needn't handle non-finite values.
Results may differ from a plain program's by a relative error of at most 0.017.
Values may be sent and summed in bfloat16 or wider, within the bound.
No kernel may reach another device: no remote copies, remote signals or barrier semaphores. Data moves between devices by JAX's collectives and lax.ppermute only.
A program may use at most 128 MiB of HBM per device.

v0:
```python
import math
import jax
import jax.numpy as jnp
from jax import lax
from jax.sharding import PartitionSpec as P

D = 2048
HEAD_DIM = 128
TOP = 8
NEW = 256
epsilon = 1e-05


def softmax_parts(queries, key_rows, values, allowed):
    scores = jnp.einsum(
        "bthe,bche->bhtc", queries, key_rows, preferred_element_type=jnp.float32
    ) / math.sqrt(HEAD_DIM)
    scores = jnp.where(allowed[:, None], scores, -1e30)
    row_max = jnp.max(scores, axis=3)
    weights = jnp.where(allowed[:, None], jnp.exp(scores - row_max[..., None]), 0.0)
    row_total = jnp.sum(weights, axis=3)
    partial_out = jnp.einsum(
        "bhtc,bche->bthe", weights.astype(jnp.bfloat16), values, preferred_element_type=jnp.float32
    )
    return (partial_out, jnp.swapaxes(row_max, 1, 2), jnp.swapaxes(row_total, 1, 2))


def combine_parts(first, second):
    out_a, max_a, total_a = first
    out_b, max_b, total_b = second
    joint = jnp.maximum(max_a, max_b)
    factor_a = jnp.exp(max_a - joint)
    factor_b = jnp.exp(max_b - joint)
    return (
        out_a * factor_a[..., None] + out_b * factor_b[..., None],
        joint,
        total_a * factor_a + total_b * factor_b,
    )


def merge_parts(pieces, maxima, totals):
    overall = jnp.max(maxima, axis=0)
    factor = jnp.exp(maxima - overall[None])
    denominator = jnp.sum(totals * factor, axis=0)
    merged = jnp.sum(pieces * factor[..., None], axis=0)
    return merged / denominator[..., None]


def dense_experts(moe_in, expert_ids, route_weights, expert_gate_up, down_full, here, experts_all):
    local_experts = expert_gate_up.shape[0]
    hidden_quarter = expert_gate_up.shape[3]
    tokens, quarter = moe_in.shape
    seq_count = experts_all // local_experts
    gate_w = jnp.sum(
        route_weights[:, :, None]
        * (expert_ids[:, :, None] == jnp.arange(experts_all, dtype=jnp.int32)[None, None, :]),
        axis=1,
    )
    gate_t = jnp.transpose(gate_w)
    gate_hi = gate_t.astype(jnp.bfloat16)
    gate_lo = (gate_t - gate_hi.astype(jnp.float32)).astype(jnp.bfloat16)
    info = jnp.concatenate([gate_hi, gate_lo], axis=0).reshape(-1, quarter)
    packed = jnp.concatenate([moe_in, info], axis=0)
    gathered = lax.all_gather(packed, "seq", axis=0, tiled=False)
    rows_q = gathered[:, :tokens].reshape(seq_count * tokens, quarter)
    info_all = gathered[:, tokens:].reshape(seq_count, 2, experts_all, tokens).astype(jnp.float32)
    gate_all = info_all[:, 0] + info_all[:, 1]
    gate_local = lax.dynamic_slice_in_dim(gate_all, here * local_experts, local_experts, axis=1)
    gate_local = jnp.transpose(gate_local, (1, 0, 2)).reshape(local_experts, seq_count * tokens)
    rows = lax.all_gather(rows_q, "tp", axis=1, tiled=True)
    gate_up = expert_gate_up.reshape(local_experts, D, 2 * hidden_quarter)
    projected = jnp.einsum("td,edf->etf", rows, gate_up, preferred_element_type=jnp.float32)
    activated = jax.nn.silu(projected[..., :hidden_quarter]) * projected[..., hidden_quarter:]
    activated = activated.astype(jnp.bfloat16).astype(jnp.float32)
    weighted = (activated * gate_local[:, :, None]).astype(jnp.bfloat16)
    weighted = lax.all_gather(weighted, "tp", axis=2, tiled=True)
    partial = jnp.einsum(
        "etf,efd->td", weighted, down_full, preferred_element_type=jnp.float32
    ).astype(jnp.bfloat16)
    partial = lax.psum_scatter(partial, "seq", scatter_dimension=0, tiled=True)
    return partial.astype(jnp.float32)


def dispatch_experts(
    moe_in, expert_ids, route_weights, expert_gate_up, expert_down, experts_all, capacity
):
    quarter = moe_in.shape[1]
    local_experts = expert_gate_up.shape[0]
    flat_ids = expert_ids.reshape(NEW * TOP)
    onehot = (flat_ids[:, None] == jnp.arange(experts_all, dtype=jnp.int32)[None, :]).astype(
        jnp.int32
    )
    ranks = jnp.sum((jnp.cumsum(onehot, axis=0) - onehot) * onehot, axis=1)
    target = (flat_ids * capacity + ranks).reshape(NEW, TOP)
    slot_ids = jnp.arange(experts_all * capacity, dtype=jnp.int32)
    selector = jnp.sum(
        (target[None, :, :] == slot_ids[:, None, None]).astype(jnp.int32), axis=2
    ).astype(jnp.bfloat16)
    send_rows = jnp.dot(selector, moe_in, preferred_element_type=jnp.float32).astype(jnp.bfloat16)
    send_rows = send_rows.reshape(experts_all, capacity, quarter)
    received = lax.all_to_all(send_rows, "seq", split_axis=0, concat_axis=1, tiled=True)
    hidden_quarter = expert_gate_up.shape[3]
    gate_up_local = expert_gate_up.reshape(local_experts, D, 2 * hidden_quarter)
    weight_rows = gate_up_local
    projected = jnp.einsum(
        "erd,edf->erf",
        lax.all_gather(received, "tp", axis=2, tiled=True),
        weight_rows,
        preferred_element_type=jnp.float32,
    )
    activated = (
        jax.nn.silu(projected[..., :hidden_quarter]) * projected[..., hidden_quarter:]
    ).astype(jnp.bfloat16)
    down_terms = jnp.einsum(
        "erf,efd->erd", activated, expert_down, preferred_element_type=jnp.float32
    )
    expert_result = lax.psum_scatter(
        down_terms.astype(jnp.bfloat16), "tp", scatter_dimension=2, tiled=True
    )
    returned = lax.all_to_all(
        expert_result, "seq", split_axis=1, concat_axis=0, tiled=True
    ).reshape(experts_all * capacity, quarter)
    picked = jnp.take(returned, target, axis=0)
    return jnp.sum(route_weights[:, :, None] * picked.astype(jnp.float32), axis=1)


def body(
    hidden,
    new_queries,
    new_keys,
    new_values,
    cache_keys,
    cache_values,
    cache_lengths,
    out_proj,
    moe_gain,
    expert_ids,
    route_weights,
    expert_gate_up,
    expert_down,
    next_gain,
    qkv_proj,
    query_gain,
    key_gain,
):
    seq_count = lax.axis_size("seq")
    here = lax.axis_index("seq")
    local_experts = expert_gate_up.shape[0]
    experts_all = local_experts * seq_count
    capacity = max(2, 3 * NEW * TOP // (2 * experts_all))
    dense = NEW <= 2 * capacity
    if dense:
        tp_here = lax.axis_index("tp")
        quarter_width = hidden.shape[1]
        down_full = lax.all_gather(expert_down, "tp", axis=1, tiled=True)
        down_full = lax.dynamic_slice_in_dim(
            down_full, tp_here * quarter_width, quarter_width, axis=2
        )
    local_width = new_queries.shape[1]
    local_heads = local_width // HEAD_DIM
    quarter = hidden.shape[1]
    own_queries = new_queries.reshape(1, NEW, local_heads, HEAD_DIM)
    own_keys = new_keys.reshape(1, NEW, local_heads, HEAD_DIM)
    own_values = new_values.reshape(1, NEW, local_heads, HEAD_DIM)
    offsets = jnp.arange(NEW, dtype=jnp.int32)
    causal = (offsets[None, :] <= offsets[:, None])[None]
    own_out, own_max, own_total = softmax_parts(own_queries, own_keys, own_values, causal)
    span = cache_keys.shape[1]
    block = min(512, span)
    my_length = lax.dynamic_index_in_dim(cache_lengths, here, 0, keepdims=False)
    block_count = (my_length + block - 1) // block
    key_blocks = cache_keys.reshape(span, local_heads, HEAD_DIM)
    value_blocks = cache_values.reshape(span, local_heads, HEAD_DIM)

    def cache_block(index, carry):
        begin = index * block
        keys_here = lax.dynamic_slice_in_dim(key_blocks, begin, block, 0)[None]
        values_here = lax.dynamic_slice_in_dim(value_blocks, begin, block, 0)[None]
        positions = begin + jnp.arange(block, dtype=jnp.int32)
        allowed = jnp.broadcast_to((positions < my_length)[None, None, :], (1, NEW, block))
        return combine_parts(carry, softmax_parts(own_queries, keys_here, values_here, allowed))

    start_parts = (
        jnp.zeros((1, NEW, local_heads, HEAD_DIM), jnp.float32),
        jnp.full((1, NEW, local_heads), -1e30, jnp.float32),
        jnp.zeros((1, NEW, local_heads), jnp.float32),
    )
    pieces, maxima, totals = lax.fori_loop(0, block_count, cache_block, start_parts)
    attended = merge_parts(
        jnp.concatenate([own_out, pieces], 0),
        jnp.concatenate([own_max, maxima], 0),
        jnp.concatenate([own_total, totals], 0),
    )
    attended = attended.reshape(NEW, local_width).astype(jnp.bfloat16)
    if dense:
        attended, down_full = lax.optimization_barrier((attended, down_full))
    attn_term = jnp.dot(attended, out_proj, preferred_element_type=jnp.float32)
    residual = hidden.astype(jnp.float32) + lax.psum_scatter(
        attn_term.astype(jnp.bfloat16), "tp", scatter_dimension=1, tiled=True
    ).astype(jnp.float32)
    square_total = lax.psum(jnp.sum(residual * residual, axis=1), "tp")
    moe_in = (residual * lax.rsqrt(square_total / D + epsilon)[:, None] * moe_gain[None, :]).astype(
        jnp.bfloat16
    )
    if dense:
        moe_term = dense_experts(
            moe_in, expert_ids, route_weights, expert_gate_up, down_full, here, experts_all
        )
    else:
        moe_term = dispatch_experts(
            moe_in, expert_ids, route_weights, expert_gate_up, expert_down, experts_all, capacity
        )
    routed = residual + moe_term
    layer_out = routed.astype(jnp.bfloat16)
    scaled = (routed * next_gain[None, :]).astype(jnp.bfloat16)
    qkv_local = qkv_proj.reshape(D, 3 * local_width)
    weight_rows = qkv_local
    mixed = jnp.dot(
        lax.all_gather(scaled, "tp", axis=1, tiled=True),
        weight_rows,
        preferred_element_type=jnp.float32,
    )
    mixed = mixed.reshape(NEW, 3, local_width)
    squares_routed = jnp.sum(routed * routed, axis=1)
    routed_total, query_raw, key_raw = lax.psum(
        (
            squares_routed,
            jnp.sum(mixed[:, 0] * mixed[:, 0], axis=1),
            jnp.sum(mixed[:, 1] * mixed[:, 1], axis=1),
        ),
        "tp",
    )
    x_scale = lax.rsqrt(routed_total / D + epsilon)
    query_pre = mixed[:, 0] * x_scale[:, None]
    key_pre = mixed[:, 1] * x_scale[:, None]
    query_total = query_raw * x_scale * x_scale
    key_total = key_raw * x_scale * x_scale
    next_query = (
        query_pre * lax.rsqrt(query_total / D + epsilon)[:, None] * query_gain[None, :]
    ).astype(jnp.bfloat16)
    next_key = (key_pre * lax.rsqrt(key_total / D + epsilon)[:, None] * key_gain[None, :]).astype(
        jnp.bfloat16
    )
    next_value = (mixed[:, 2] * x_scale[:, None]).astype(jnp.bfloat16)
    return (layer_out, next_query, next_key, next_value)


def solution(mesh):
    return jax.shard_map(
        body,
        mesh=mesh,
        in_specs=(
            P("seq", "tp"),
            P("seq", "tp"),
            P("seq", "tp"),
            P("seq", "tp"),
            P("seq", None, "tp"),
            P("seq", None, "tp"),
            P(),
            P("tp", None),
            P("tp"),
            P("seq", None),
            P("seq", None),
            P("seq", None, None, "tp"),
            P("seq", "tp", None),
            P("tp"),
            P(None, None, "tp"),
            P("tp"),
            P("tp"),
        ),
        out_specs=(P("seq", "tp"), P("seq", "tp"), P("seq", "tp"), P("seq", "tp")),
        check_vma=False,
    )
```

profile of v0, /device:TPU:0, one launch (start us, length us, event | category | flops | bytes accessed | tf_op | source)
XLA Modules:
  0.0 412.0 jit_solution(3361592434585957795)
XLA Ops:
  9.6 6.4 %copy.95 = bf16[1,4096,512]{1,2,0:T(8,128)(2,1)} copy(bf16[1,4096,512]{2,1,0:T(8,128)(2,1)} %param.23) | data formatting | bytes 8388608 | tf_op args[4]
  16.0 6.6 %copy.97 = bf16[1,4096,512]{1,2,0:T(8,128)(2,1)} copy(bf16[1,4096,512]{2,1,0:T(8,128)(2,1)} %param.24) | data formatting | bytes 8388608 | tf_op args[5]
  22.7 28.9 %while.14 = (s32[]{:T(128)}, f32[1,256,4,128]{1,3,2,0:T(8,128)S(1)}, f32[1,256,4]{1,2,0:T(4,128)S(1)}, f32[1,256,4]{1,2,0:T(4,128)S(1)}, s32[]{:T(128)}, /*index...) while((s32[]{:T(128)}, ...), condition=%wide.region_4.5_spmd, body=%wide.region_1.4_spmd.sunk | while | flops 275651584 | bytes 8731323 | solution.py:188
  25.7 1.8 fusion.83
  40.1 1.8 fusion.83
  54.5 16.1 %all-gather.7.cloned.1.call-done = bf16[2,1024,2048]{2,1,0:T(8,128)(2,1)} async-done(((bf16[2,256,2048]{2,1,0:T(8,128)(2,1)}), bf16[2,1024,2048]{2,1,0:T(8,128)(2,1)}) %all-gather.7.cloned.1.call-update) | async-done | bytes 8388624 | tf_op jit(solution)/shard_map/all_gather | solution.py:155
  70.6 3.0 constant_dynamic-slice_fusion
  75.5 24.9 %reduce-scatter.3.cloned.1.call-done = bf16[256,512]{1,0:T(8,128)(2,1)} async-done(((bf16[256,2048]{1,0:T(8,128)(2,1)}), bf16[256,512]{1,0:T(8,128)(2,1)}) %reduce-scatter.3.cloned.1.call-update) | async-done | bytes 262160 | tf_op jit(solution)/shard_map/reduce_scatter | solution.py:198
  101.6 5.8 %psum.28 = f32[256]{0:T(256)S(1)} all-reduce(f32[256]{0:T(256)S(1)} %multiply_reduce_fusion.3), channel_id=1, replica_groups=mesh['seq'=8,'tp'=4] {'tp'}, use_global_device_ids=true, to_apply=%region_10.11 | all-reduce | flops 256 | bytes 2048 | tf_op jit(solution)/shard_map/psum | solution.py:201
  109.2 51.9 %all-gather.15.cloned.1.call-done = bf16[2176,512]{1,0:T(8,128)(2,1)} async-done(((bf16[272,512]{1,0:T(8,128)(2,1)}), bf16[2176,512]{1,0:T(8,128)(2,1)}) %all-gather.15.cloned.1.call-update) | async-done | bytes 2228240 | tf_op jit(solution)/shard_map/all_gather | solution.py:64
  161.1 3.1 slice.40
  164.2 7.8 %reshape.166 = bf16[2,2048,512]{2,1,0:T(8,128)(2,1)} reshape(bf16[2,2048,2,256]{3,2,1,0:T(2,128)(2,1)} %param.30) | data formatting | bytes 8388608 | tf_op jit(solution)/shard_map/reshape | solution.py:71
  173.1 48.0 %all-gather.9.cloned.1.call-done = bf16[2048,2048]{1,0:T(8,128)(2,1)} async-done(((bf16[2048,512]{1,0:T(8,128)(2,1)}), bf16[2048,2048]{1,0:T(8,128)(2,1)}) %all-gather.9.cloned.1.call-update) | async-done | bytes 8388624 | tf_op jit(solution)/shard_map/all_gather | solution.py:70
  221.1 12.4 %fusion.29 = f32[2,2048,512]{2,1,0:T(8,128)S(1)} fusion(bf16[2,2048,512]{2,1,0:T(8,128)(2,1)} %reshape.166, bf16[2048,2048]{1,0:T(8,128)(2,1)} %all-gather.9.cloned.1.call-done), kind=kOutput, calls=%fused_computation.37 | convolution fusion | flops 8589934592 | bytes 20971520 | tf_op jit(solution)/shard_map/td,edf->etf/dot_general | solution.py:72
  233.6 2.2 multiply_convert_fusion
  236.0 59.3 %all-gather.11.cloned.1.call-done = bf16[2,2048,1024]{2,1,0:T(8,128)(2,1)} async-done(((bf16[2,2048,256]{2,1,0:T(8,128)(2,1)}), bf16[2,2048,1024]{2,1,0:T(8,128)(2,1)}) %all-gather.11.cloned.1.call-update) | async-done | bytes 8388624 | tf_op jit(solution)/shard_map/all_gather | solution.py:76
  295.3 9.1 %bitcast_convert_fusion = bf16[2048,512]{1,0:T(8,128)(2,1)} fusion(bf16[2,2048,1024]{2,1,0:T(8,128)(2,1)} %all-gather.11.cloned.1.call-done, bf16[2,1024,512]{2,1,0:T(8,128)(2,1)S(1)} %copy-done.5), kind=kOutput, calls=%fused_computation.40 | convolution fusion | flops 4296015872 | bytes 12582912 | tf_op jit(solution)/shard_map/etf,efd->td/dot_general | solution.py:77
  304.5 68.0 %reduce-scatter.5.cloned.1.call-done = bf16[256,512]{1,0:T(8,128)(2,1)} async-done(((bf16[2048,512]{1,0:T(8,128)(2,1)}), bf16[256,512]{1,0:T(8,128)(2,1)}) %reduce-scatter.5.cloned.1.call-update) | async-done | bytes 262160 | tf_op jit(solution)/shard_map/reduce_scatter | solution.py:80
  372.5 1.9 multiply_reduce_fusion.2
  374.4 8.9 %copy.103 = bf16[2048,3,512]{0,2,1:T(8,128)(2,1)} copy(bf16[2048,3,512]{2,0,1:T(8,128)(2,1)} %param.33) | data formatting | bytes 12582912 | tf_op args[14]
  383.3 7.1 %all-gather.13.cloned.1.call-done = bf16[256,2048]{1,0:T(8,128)(2,1)} async-done(((bf16[256,512]{1,0:T(8,128)(2,1)}), bf16[256,2048]{1,0:T(8,128)(2,1)}) %all-gather.13.cloned.1.call-update) | async-done | bytes 1048592 | tf_op jit(solution)/shard_map/all_gather | solution.py:219
  390.4 5.1 %fusion.27 = f32[256,3,512]{2,0,1:T(8,128)S(1)} fusion(bf16[2048,3,512]{0,2,1:T(8,128)(2,1)} %copy.103, bf16[256,2048]{1,0:T(8,128)(2,1)} %all-gather.13.cloned.1.call-done), kind=kOutput, calls=%fused_computation.35 | convolution fusion | flops 1610612736 | bytes 8912896 | tf_op jit(solution)/shard_map/dot_general | solution.py:218
  396.8 5.9 %all-reduce = (f32[256]{0:T(256)S(1)}, f32[256]{0:T(256)S(1)}, f32[256]{0:T(256)S(1)}) all-reduce(f32[256]{0:T(256)S(1)} %get-tuple-element.107, f32[256]{0:T(256)S(1)} %get-tuple-element.142, f32[256]{0:T(256)S(1)} %get-tuple-element.106), channel_id=1, replica_groups=mesh['seq'=8,'tp'=4] {'tp'}, use_global_device_ids=true, to_apply=%region_16.17 | all-reduce | flops 768 | bytes 6144 | tf_op jit(solution)/shard_map/psum | solution.py:225
  402.7 2.4 fusion.40
  (117 shorter events, 37.0 us)
Async XLA Ops:
  7.2 66.5 %copy-start = (bf16[512,2048]{1,0:T(8,128)(2,1)S(1)}, bf16[512,2048]{1,0:T(8,128)(2,1)}, u32[]{:S(2)}) copy-start(bf16[512,2048]{1,0:T(8,128)(2,1)} %param.26) | copy-start | bytes 6291460
  7.2 0.8 copy-start.14
  7.2 2.1 copy-start.6
  7.2 63.4 %all-gather.7.cloned.1.call-start = ((), (), s32[]{:S(2)}) async-start(), calls=%async_computation.2 | async-start | bytes 10485760 | tf_op jit(solution)/shard_map/all_gather | solution.py:155
  7.9 92.5 %reduce-scatter.3.cloned.1.call-start = ((), (), s32[]{:S(2)}) async-start(), calls=%async_computation.3 | async-start | bytes 1310720 | tf_op jit(solution)/shard_map/reduce_scatter | solution.py:198
  51.8 1.6 copy-start.7
  73.6 1.8 copy-start.8
  73.6 1.8 copy-start.9
  73.6 26.8 %copy-start.3 = (bf16[256,512]{1,0:T(8,128)(2,1)S(1)}, bf16[256,512]{1,0:T(8,128)(2,1)}, u32[]{:S(2)}) copy-start(bf16[256,512]{1,0:T(8,128)(2,1)} %param.19) | copy-start | bytes 786436
  73.7 33.7 %copy-start.10 = (f32[512]{0:T(512)S(1)}, f32[512]{0:T(512)}, u32[]{:S(2)}) copy-start(f32[512]{0:T(512)} %param.27) | copy-start | bytes 6148
  75.4 85.7 %all-gather.15.cloned.1.call-start = ((), (), s32[]{:S(2)}) async-start(), calls=%async_computation.8 | async-start | bytes 2506752 | tf_op jit(solution)/shard_map/all_gather | solution.py:64
  109.1 111.9 %all-gather.9.cloned.1.call-start = ((), (), s32[]{:S(2)}) async-start(), calls=%async_computation.4 | async-start | bytes 10485760 | tf_op jit(solution)/shard_map/all_gather | solution.py:70
  164.1 131.2 %all-gather.11.cloned.1.call-start = ((), (), s32[]{:S(2)}) async-start(), calls=%async_computation.5 | async-start | bytes 10485760 | tf_op jit(solution)/shard_map/all_gather | solution.py:76
  235.7 59.6 %copy-start.5 = (bf16[2,1024,512]{2,1,0:T(8,128)(2,1)S(1)}, bf16[2,1024,512]{2,1,0:T(8,128)(2,1)}, u32[]{:S(2)}) copy-start(bf16[2,1024,512]{2,1,0:T(8,128)(2,1)} %constant_dynamic-slice_fusion) | copy-start | bytes 6291460
  235.8 136.7 %reduce-scatter.5.cloned.1.call-start = ((), (), s32[]{:S(2)}) async-start(), calls=%async_computation.6 | async-start | bytes 2359296 | tf_op jit(solution)/shard_map/reduce_scatter | solution.py:80
  304.4 68.0 %copy-start.4 = (bf16[256,512]{1,0:T(8,128)(2,1)S(1)}, bf16[256,512]{1,0:T(8,128)(2,1)}, u32[]{:S(2)}) copy-start(bf16[256,512]{1,0:T(8,128)(2,1)} %reduce-scatter.3.cloned.1.call-done) | copy-start | bytes 786436
  304.4 68.0 %copy-start.11 = (f32[512]{0:T(512)S(1)}, f32[512]{0:T(512)}, u32[]{:S(2)}) copy-start(f32[512]{0:T(512)} %param.32) | copy-start | bytes 6148
  304.5 86.0 %all-gather.13.cloned.1.call-start = ((), (), s32[]{:S(2)}) async-start(), calls=%async_computation.7 | async-start | bytes 1310720 | tf_op jit(solution)/shard_map/all_gather | solution.py:219
  383.3 19.4 %copy-start.12 = (f32[512]{0:T(512)S(1)}, f32[512]{0:T(512)}, u32[]{:S(2)}) copy-start(f32[512]{0:T(512)} %param.35) | copy-start | bytes 6148
  383.3 19.4 %copy-start.13 = (f32[512]{0:T(512)S(1)}, f32[512]{0:T(512)}, u32[]{:S(2)}) copy-start(f32[512]{0:T(512)} %param.34) | copy-start | bytes 6148
  390.4 14.7 %copy-start.1 = (bf16[512,2048]{1,0:T(8,128)(2,1)S(1)}, bf16[512,2048]{1,0:T(8,128)(2,1)}, u32[]{:S(2)}) copy-start(bf16[512,2048]{1,0:T(8,128)(2,1)} %param.26) | copy-start | bytes 6291460
  395.5 1.2 copy-start.2
Sparse Core Ops, SparseCore 0:
  9.6 60.9 all-gather.6
  75.5 24.8 reduce-scatter.2
  109.3 51.7 all-gather.14
  164.3 56.7 all-gather.8
  235.9 59.3 all-gather.10
  304.6 67.8 reduce-scatter.4
  374.7 15.6 all-gather.12
where the time goes:
time: 414 us; the launch traced here: 412 us
  waiting for transfers between devices  276 us (67%)
  matrix products  50.8 us (12%)
  local copies, waits for them, and re-layouts  38.4 us (9%)
  other arithmetic  19.2 us (5%)
  between operations  15.1 us (4%)
  blocking collectives  11.7 us (3%)
    reduce_scatter x1, waiting for transfers between devices, dense_experts(): partial = lax.psum_scatter(partial, 'seq', scatter_dimension=0, tiled=True)  68 us
    all_gather x1, waiting for transfers between devices, dense_experts(): weighted = lax.all_gather(weighted, 'tp', axis=2, tiled=True)  59.3 us
    all_gather x1, waiting for transfers between devices, dense_experts(): gathered = lax.all_gather(packed, 'seq', axis=0, tiled=False)  51.9 us
    all_gather x1, waiting for transfers between devices, dense_experts(): rows = lax.all_gather(rows_q, 'tp', axis=1, tiled=True)  48 us
    reduce_scatter x1, waiting for transfers between devices, body(): lax.psum_scatter(attn_term.astype(jnp.bfloat16), 'tp', scatter_dimension=...  24.9 us
    unnamed x35, local copies, waits for them, and re-layouts  23.3 us
    all_gather x1, waiting for transfers between devices, body(): down_full = lax.all_gather(expert_down, 'tp', axis=1, tiled=True)  16.1 us
    dot_general x1, matrix products, dense_experts(): jnp.einsum('td,edf->etf', rows, gate_up, preferred_element_type=jnp.float32)  12.4 us
  transfers between devices with their start and end apart: 7, of which 7 were waited for; matrix products, arithmetic and copies ran while one was open for 15% of the time, Pallas kernels for 0%

commit v1 on v0

--- a/solution.py
+++ b/solution.py
@@ -9,6 +9,19 @@
 TOP = 8
 NEW = 256
 epsilon = 1e-05
+
+
+def ring_gather(x, axis, dim):
+    ways = lax.axis_size(axis)
+    up = [(d, (d + 1) % ways) for d in range(ways)]
+    down = [(d, (d - 1) % ways) for d in range(ways)]
+    earlier, later = ([x], [x])
+    for _ in range(ways // 2):
+        earlier.append(lax.ppermute(earlier[-1], axis, up))
+    for _ in range((ways - 1) // 2):
+        later.append(lax.ppermute(later[-1], axis, down))
+    line = jnp.concatenate([*earlier[::-1], *later[1:]], axis=dim)
+    return jnp.roll(line, (lax.axis_index(axis) - ways // 2) * x.shape[dim], axis=dim)
 
 
 def softmax_parts(queries, key_rows, values, allowed):
@@ -73,7 +86,7 @@
     activated = jax.nn.silu(projected[..., :hidden_quarter]) * projected[..., hidden_quarter:]
     activated = activated.astype(jnp.bfloat16).astype(jnp.float32)
     weighted = (activated * gate_local[:, :, None]).astype(jnp.bfloat16)
-    weighted = lax.all_gather(weighted, "tp", axis=2, tiled=True)
+    weighted = ring_gather(weighted, "tp", 2)
     partial = jnp.einsum(
         "etf,efd->td", weighted, down_full, preferred_element_type=jnp.float32
     ).astype(jnp.bfloat16)

time: 414 us -> 440 us (1.063)
  local copies, waits for them, and re-layouts: 38.4 us -> 51.2 us
  other arithmetic: 19.2 us -> 26.3 us
  waiting for transfers between devices: 276 us -> 282 us
    ppermute x0 -> x3, waiting for transfers between devices: none -> 70.9 us  [the longest x2 70.9 us: ring_gather(): earlier.append(lax.ppermute(earlier[-1], axis, up))]
    all_gather x1 -> x0, waiting for transfers between devices: 59.3 us -> none  [dense_experts(): weighted = lax.all_gather(weighted, 'tp', axis=2, tiled=True)]
    unnamed x35 -> x42, local copies, waits for them, and re-layouts: 23.3 us -> 29.8 us
    unnamed x0 -> x3, other arithmetic: none -> 6.27 us
  transfers between devices with their start and end apart: 7 -> 9, of which waited for: 7 -> 8; matrix products, arithmetic and copies ran while one was open for 15% -> 17% of each run, Pallas kernels for 0% -> 0%
where the time goes in v1:
time: 440 us; the launch traced here: 438 us
  waiting for transfers between devices  282 us (64%)
  local copies, waits for them, and re-layouts  51.2 us (12%)
  matrix products  48.5 us (11%)
  other arithmetic  26.3 us (6%)
  between operations  15.2 us (3%)
  blocking collectives  11.7 us (3%)
    ppermute x2, waiting for transfers between devices, ring_gather(): earlier.append(lax.ppermute(earlier[-1], axis, up))  70.9 us
    reduce_scatter x1, waiting for transfers between devices, dense_experts(): partial = lax.psum_scatter(partial, 'seq', scatter_dimension=0, tiled=True)  67.7 us
    all_gather x1, waiting for transfers between devices, dense_experts(): gathered = lax.all_gather(packed, 'seq', axis=0, tiled=False)  51.9 us
    all_gather x1, waiting for transfers between devices, dense_experts(): rows = lax.all_gather(rows_q, 'tp', axis=1, tiled=True)  44.4 us
    unnamed x42, local copies, waits for them, and re-layouts  29.8 us
    reduce_scatter x1, waiting for transfers between devices, body(): lax.psum_scatter(attn_term.astype(jnp.bfloat16), 'tp', scatter_dimension=...  24.9 us
    all_gather x1, waiting for transfers between devices, body(): down_full = lax.all_gather(expert_down, 'tp', axis=1, tiled=True)  14.6 us
    dot_general x1, matrix products, dense_experts(): jnp.einsum('td,edf->etf', rows, gate_up, preferred_element_type=jnp.float32)  12.5 us
  transfers between devices with their start and end apart: 9, of which 8 were waited for; matrix products, arithmetic and copies ran while one was open for 17% of the time, Pallas kernels for 0%

profile of v1, /device:TPU:0, one launch (start us, length us, event | category | flops | bytes accessed | tf_op | source)
XLA Modules:
  0.0 437.6 jit_solution(8751061556165997770)
XLA Ops:
  9.9 6.4 %copy.105 = bf16[1,4096,512]{1,2,0:T(8,128)(2,1)} copy(bf16[1,4096,512]{2,1,0:T(8,128)(2,1)} %param.23) | data formatting | bytes 8388608 | tf_op args[4]
  16.6 6.5 %copy.107 = bf16[1,4096,512]{1,2,0:T(8,128)(2,1)} copy(bf16[1,4096,512]{2,1,0:T(8,128)(2,1)} %param.24) | data formatting | bytes 8388608 | tf_op args[5]
  23.2 28.9 %while.14 = (s32[]{:T(128)}, f32[1,256,4,128]{1,3,2,0:T(8,128)S(1)}, f32[1,256,4]{1,2,0:T(4,128)S(1)}, f32[1,256,4]{1,2,0:T(4,128)S(1)}, s32[]{:T(128)}, /*index...) while((s32[]{:T(128)}, ...), condition=%wide.region_4.5_spmd, body=%wide.region_1.4_spmd.sunk | while | flops 275651584 | bytes 8731331 | solution.py:201
  56.0 14.6 %all-gather.6.cloned.1.call-done = bf16[2,1024,2048]{2,1,0:T(8,128)(2,1)} async-done(((bf16[2,256,2048]{2,1,0:T(8,128)(2,1)}), bf16[2,1024,2048]{2,1,0:T(8,128)(2,1)}) %all-gather.6.cloned.1.call-update) | async-done | bytes 8388624 | tf_op jit(solution)/shard_map/all_gather | solution.py:168
  70.6 3.0 constant_dynamic-slice_fusion
  75.5 24.9 %reduce-scatter.3.cloned.1.call-done = bf16[256,512]{1,0:T(8,128)(2,1)} async-done(((bf16[256,2048]{1,0:T(8,128)(2,1)}), bf16[256,512]{1,0:T(8,128)(2,1)}) %reduce-scatter.3.cloned.1.call-update) | async-done | bytes 262160 | tf_op jit(solution)/shard_map/reduce_scatter | solution.py:211
  101.5 5.8 %psum.28 = f32[256]{0:T(256)S(1)} all-reduce(f32[256]{0:T(256)S(1)} %multiply_reduce_fusion.3), channel_id=1, replica_groups=mesh['seq'=8,'tp'=4] {'tp'}, use_global_device_ids=true, to_apply=%region_10.11 | all-reduce | flops 256 | bytes 2048 | tf_op jit(solution)/shard_map/psum | solution.py:214
  109.1 51.9 %all-gather.12.cloned.1.call-done = bf16[2176,512]{1,0:T(8,128)(2,1)} async-done(((bf16[272,512]{1,0:T(8,128)(2,1)}), bf16[2176,512]{1,0:T(8,128)(2,1)}) %all-gather.12.cloned.1.call-update) | async-done | bytes 2228240 | tf_op jit(solution)/shard_map/all_gather | solution.py:77
  161.0 3.1 slice.40
  164.1 11.5 %copy.120 = bf16[2,2048,2,256]{1,3,2,0:T(8,128)(2,1)} copy(bf16[2,2048,2,256]{3,2,1,0:T(2,128)(2,1)} %param.30) | data formatting | bytes 8388608 | tf_op jit(solution)/shard_map/reshape | solution.py:84
  176.7 44.4 %all-gather.8.cloned.1.call-done = bf16[2048,2048]{1,0:T(8,128)(2,1)} async-done(((bf16[2048,512]{1,0:T(8,128)(2,1)}), bf16[2048,2048]{1,0:T(8,128)(2,1)}) %all-gather.8.cloned.1.call-update) | async-done | bytes 8388624 | tf_op jit(solution)/shard_map/all_gather | solution.py:83
  221.1 12.5 %fusion.31 = f32[2,2048,512]{1,2,0:T(8,128)S(1)} fusion(bf16[2,2048,512]{1,2,0:T(8,128)(2,1)} %bitcast.168, bf16[2048,2048]{1,0:T(8,128)(2,1)} %all-gather.8.cloned.1.call-done), kind=kOutput, calls=%fused_computation.39 | convolution fusion | flops 8589934592 | bytes 20971520 | tf_op jit(solution)/shard_map/td,edf->etf/dot_general | solution.py:85
  233.6 3.1 multiply_convert_fusion
  237.8 25.4 %collective-permute-done = bf16[2,2048,256]{1,2,0:T(8,128)(2,1)S(1)} collective-permute-done((bf16[2,2048,256]{1,2,0:T(8,128)(2,1)}, bf16[2,2048,256]{1,2,0:T(8,128)(2,1)S(1)}, u32[]{:S(2)}, u32[]{:S(2)}) %collective-permute-start) | collective-permute-done | bytes 2097184 | tf_op jit(solution)/shard_map/ppermute | solution.py:20
  264.9 45.5 %collective-permute-done.1 = bf16[2,2048,256]{1,2,0:T(8,128)(2,1)} collective-permute-done((bf16[2,2048,256]{1,2,0:T(8,128)(2,1)S(1)}, bf16[2,2048,256]{1,2,0:T(8,128)(2,1)}, u32[]{:S(2)}, u32[]{:S(2)}) %collective-permute-start.1) | collective-permute-done | bytes 2097184 | tf_op jit(solution)/shard_map/ppermute | solution.py:20
  312.3 4.9 %constant_dynamic-update-slice_fusion.5 = bf16[2,2048,2048]{1,2,0:T(8,128)(2,1)S(1)} fusion(bf16[2,2048,2048]{1,2,0:T(8,128)(2,1)S(1)} %constant_dynamic-update-slice_fusion.6, f32[2,2048]{1,0:T(2,128)S(1)} %bitcast.174, f32[2,2048,512]{1,2,0:T(8,128)} %copy-done.2), kind=kLoop, calls=%fused_computation.90 | loop fusion | flops 9437184 | bytes 10502144
  324.6 5.8 %bitcast_convert_fusion = bf16[2048,512]{1,0:T(8,128)(2,1)} fusion(bf16[2,1024,512]{2,1,0:T(8,128)(2,1)S(1)} %copy-done.6, bf16[2,2048,2048]{1,2,0:T(8,128)(2,1)S(1)} %constant_dynamic-update-slice_fusion, s32[]{:T(128)S(6)} %select_n.59), kind=kOutput, calls=%fused_computation.42 | convolution fusion | flops 4296015872 | bytes 12582916 | tf_op jit(solution)/shard_map/etf,efd->td/dot_general | solution.py:90
  330.5 67.7 %reduce-scatter.5.cloned.1.call-done = bf16[256,512]{1,0:T(8,128)(2,1)} async-done(((bf16[2048,512]{1,0:T(8,128)(2,1)}), bf16[256,512]{1,0:T(8,128)(2,1)}) %reduce-scatter.5.cloned.1.call-update) | async-done | bytes 262160 | tf_op jit(solution)/shard_map/reduce_scatter | solution.py:93
  398.2 1.9 multiply_reduce_fusion.2
  400.1 8.8 %copy.115 = bf16[2048,3,512]{0,2,1:T(8,128)(2,1)} copy(bf16[2048,3,512]{2,0,1:T(8,128)(2,1)} %param.33) | data formatting | bytes 12582912 | tf_op args[14]
  408.9 7.1 %all-gather.10.cloned.1.call-done = bf16[256,2048]{1,0:T(8,128)(2,1)} async-done(((bf16[256,512]{1,0:T(8,128)(2,1)}), bf16[256,2048]{1,0:T(8,128)(2,1)}) %all-gather.10.cloned.1.call-update) | async-done | bytes 1048592 | tf_op jit(solution)/shard_map/all_gather | solution.py:232
  416.0 5.1 %fusion.29 = f32[256,3,512]{2,0,1:T(8,128)S(1)} fusion(bf16[2048,3,512]{0,2,1:T(8,128)(2,1)} %copy.115, bf16[256,2048]{1,0:T(8,128)(2,1)} %all-gather.10.cloned.1.call-done), kind=kOutput, calls=%fused_computation.37 | convolution fusion | flops 1610612736 | bytes 8912896 | tf_op jit(solution)/shard_map/dot_general | solution.py:231
  422.4 5.9 %all-reduce = (f32[256]{0:T(256)S(1)}, f32[256]{0:T(256)S(1)}, f32[256]{0:T(256)S(1)}) all-reduce(f32[256]{0:T(256)S(1)} %get-tuple-element.107, f32[256]{0:T(256)S(1)} %get-tuple-element.142, f32[256]{0:T(256)S(1)} %get-tuple-element.106), channel_id=1, replica_groups=mesh['seq'=8,'tp'=4] {'tp'}, use_global_device_ids=true, to_apply=%region_16.17 | all-reduce | flops 768 | bytes 6144 | tf_op jit(solution)/shard_map/psum | solution.py:238
  428.3 2.4 fusion.44
  (131 shorter events, 53.9 us)
Async XLA Ops:
  7.2 66.5 %copy-start = (bf16[512,2048]{1,0:T(8,128)(2,1)S(1)}, bf16[512,2048]{1,0:T(8,128)(2,1)}, u32[]{:S(2)}) copy-start(bf16[512,2048]{1,0:T(8,128)(2,1)} %param.26) | copy-start | bytes 6291460
  7.2 63.4 %all-gather.6.cloned.1.call-start = ((), (), s32[]{:S(2)}) async-start(), calls=%async_computation.2 | async-start | bytes 10485760 | tf_op jit(solution)/shard_map/all_gather | solution.py:168
  7.9 92.5 %reduce-scatter.3.cloned.1.call-start = ((), (), s32[]{:S(2)}) async-start(), calls=%async_computation.3 | async-start | bytes 1310720 | tf_op jit(solution)/shard_map/reduce_scatter | solution.py:211
  9.9 6.4 %copy-start.7 = (bf16[256,512]{1,0:T(8,128)(2,1)S(1)}, bf16[256,512]{1,0:T(8,128)(2,1)}, u32[]{:S(2)}) copy-start(bf16[256,512]{1,0:T(8,128)(2,1)} %param.20) | copy-start | bytes 786436
  56.0 19.4 %copy-start.8 = (f32[256,8]{0,1:T(8,128)S(1)}, f32[256,8]{0,1:T(8,128)}, u32[]{:S(2)}) copy-start(f32[256,8]{0,1:T(8,128)} %param.29) | copy-start | bytes 24580
  56.0 19.4 %copy-start.9 = (s32[256,8]{0,1:T(8,128)S(1)}, s32[256,8]{0,1:T(8,128)}, u32[]{:S(2)}) copy-start(s32[256,8]{0,1:T(8,128)} %param.28) | copy-start | bytes 24580
  56.0 44.4 %copy-start.4 = (bf16[256,512]{1,0:T(8,128)(2,1)S(1)}, bf16[256,512]{1,0:T(8,128)(2,1)}, u32[]{:S(2)}) copy-start(bf16[256,512]{1,0:T(8,128)(2,1)} %param.19) | copy-start | bytes 786436
  56.0 51.2 %copy-start.10 = (f32[512]{0:T(512)S(1)}, f32[512]{0:T(512)}, u32[]{:S(2)}) copy-start(f32[512]{0:T(512)} %param.27) | copy-start | bytes 6148
  75.3 85.7 %all-gather.12.cloned.1.call-start = ((), (), s32[]{:S(2)}) async-start(), calls=%async_computation.7 | async-start | bytes 2506752 | tf_op jit(solution)/shard_map/all_gather | solution.py:77
  109.1 112.0 %all-gather.8.cloned.1.call-start = ((), (), s32[]{:S(2)}) async-start(), calls=%async_computation.4 | async-start | bytes 10485760 | tf_op jit(solution)/shard_map/all_gather | solution.py:83
  164.1 234.1 %reduce-scatter.5.cloned.1.call-start = ((), (), s32[]{:S(2)}) async-start(), calls=%async_computation.5 | async-start | bytes 2359296 | tf_op jit(solution)/shard_map/reduce_scatter | solution.py:93
  233.6 3.9 copy-start.2
  237.5 25.7 %collective-permute-start = (bf16[2,2048,256]{1,2,0:T(8,128)(2,1)}, bf16[2,2048,256]{1,2,0:T(8,128)(2,1)S(1)}, u32[]{:S(2)}, u32[]{:S(2)}) collective-permute-start(bf16[2,2048,256]{1,2,0:T(8,128)(2,1)} %multiply_convert_fusion), channel_id=1, source_target_pairs={{0,1},{1,2},{2,3},{3,0},{4,5},{5,6},{6,7},{7,4},{8,9},{9,10},{10,1... | collective-permute-start | bytes 6291464 | tf_op jit(solution)/shard_map/ppermute | solution.py:20
  263.2 47.2 %collective-permute-start.1 = (bf16[2,2048,256]{1,2,0:T(8,128)(2,1)S(1)}, bf16[2,2048,256]{1,2,0:T(8,128)(2,1)}, u32[]{:S(2)}, u32[]{:S(2)}) collective-permute-start(bf16[2,2048,256]{1,2,0:T(8,128)(2,1)S(1)} %collective-permute-done), channel_id=1, source_target_pairs={{0,1},{1,2},{2,3},{3,0},{4,5},{5,6},{6,7},{7,4},{8,9},{9,10},{10,1... | collective-permute-start | bytes 6291464 | tf_op jit(solution)/shard_map/ppermute | solution.py:20
  263.2 54.0 %collective-permute-start.2 = (bf16[2,2048,256]{1,2,0:T(8,128)(2,1)}, bf16[2,2048,256]{1,2,0:T(8,128)(2,1)}, u32[]{:S(2)}, u32[]{:S(2)}) collective-permute-start(bf16[2,2048,256]{1,2,0:T(8,128)(2,1)} %multiply_convert_fusion), channel_id=1, source_target_pairs={{0,3},{1,0},{2,1},{3,2},{4,7},{5,4},{6,5},{7,6},{8,11},{9,8},{10,9... | collective-permute-start | bytes 6291464 | tf_op jit(solution)/shard_map/ppermute | solution.py:22
  312.3 8.7 %slice-start = ((s8[8388608]{0:T(1024)(128)(4,1)}), s8[4194304]{0:T(1024)(128)(4,1)S(1)}, s32[]{:S(2)}) async-start(s8[8388608]{0:T(1024)(128)(4,1)} %bitcast.163), calls=%async_computation.8 | async-start | bytes 8388608
  317.2 3.8 slice-start.1
  322.4 2.2 copy-start.6
  324.6 73.6 %copy-start.5 = (bf16[256,512]{1,0:T(8,128)(2,1)S(1)}, bf16[256,512]{1,0:T(8,128)(2,1)}, u32[]{:S(2)}) copy-start(bf16[256,512]{1,0:T(8,128)(2,1)} %reduce-scatter.3.cloned.1.call-done) | copy-start | bytes 786436
  324.6 73.6 %copy-start.11 = (f32[512]{0:T(512)S(1)}, f32[512]{0:T(512)}, u32[]{:S(2)}) copy-start(f32[512]{0:T(512)} %param.32) | copy-start | bytes 6148
  330.4 85.5 %all-gather.10.cloned.1.call-start = ((), (), s32[]{:S(2)}) async-start(), calls=%async_computation.6 | async-start | bytes 1310720 | tf_op jit(solution)/shard_map/all_gather | solution.py:232
  408.9 19.4 %copy-start.12 = (f32[512]{0:T(512)S(1)}, f32[512]{0:T(512)}, u32[]{:S(2)}) copy-start(f32[512]{0:T(512)} %param.35) | copy-start | bytes 6148
  408.9 19.4 %copy-start.13 = (f32[512]{0:T(512)S(1)}, f32[512]{0:T(512)}, u32[]{:S(2)}) copy-start(f32[512]{0:T(512)} %param.34) | copy-start | bytes 6148
  416.0 14.7 %copy-start.1 = (bf16[512,2048]{1,0:T(8,128)(2,1)S(1)}, bf16[512,2048]{1,0:T(8,128)(2,1)}, u32[]{:S(2)}) copy-start(bf16[512,2048]{1,0:T(8,128)(2,1)} %param.26) | copy-start | bytes 6291460
  (1 other events, 1.1 us)
Sparse Core Ops, SparseCore 0:
  9.6 60.9 all-gather.5
  75.5 24.8 reduce-scatter.2
  109.2 51.7 all-gather.11
  164.2 56.7 all-gather.7
  330.6 67.5 reduce-scatter.4
  400.2 15.7 all-gather.9
